TPU v7x, 32 devices: a whole 2x2x4 slice. The times are simulated.
32 devices in a mesh: pair: 4 (over z), gen: 8 (over y, x, core).
Axes of the slice: x: 2, y: 2, z: 4, core: 2. Of those that a mesh axis runs over, the one named last changes fastest.
Arguments:
- tokens: bfloat16 [32768, 2048], P(('pair', 'gen')), may hold values from -6 to 6
- cotangent: bfloat16 [32768, 256], P(('pair', 'gen')), may hold values from -6 to 6
- block_pair: int32 [32, 1], replicated, may hold values from 0 to 15
- src_lang: int32 [16], replicated, may hold values from 0 to 95
- tgt_lang: int32 [16], replicated, may hold values from 0 to 95
- lang_embed: float32 [96, 512], P(None, 'pair'), may hold values from -5 to 5
- generator: bfloat16 [512, 524288], P('pair', 'gen'), may hold values from -0.005859375 to 0.005859375
Outputs:
- grad_tokens: bfloat16 [32768, 2048], P(('pair', 'gen'))
- grad_generator: bfloat16 [512, 524288], P('pair', 'gen')
- grad_embed: float32 [96, 512], P(None, 'pair')
Inputs may be any that keep to these rules, and one draw needn't show every extreme that they name: `block_pair`: every pair owns at least one block; block counts per pair are uneven.
All inputs are finite; a program needn't handle non-finite values.
Results may differ from a plain program's by a relative error of at most 0.007.
Values may be sent and summed in bfloat16 or wider, within the bound.
No kernel may reach another device: no remote copies, remote signals or barrier semaphores. Data moves between devices by JAX's collectives and lax.ppermute only.
A program may use at most 128 MiB of HBM per device.

v0:
```python
import jax
import jax.numpy as jnp
from jax import lax
from jax.sharding import PartitionSpec as P

BLK = 1024


def shards(tokens, cotangent, block_pair, src_lang, tgt_lang, lang_embed, generator):
    gen_count = lax.axis_size("gen")
    pair_index = lax.axis_index("pair")
    blocks_here = tokens.shape[0] // BLK
    model_width = tokens.shape[1]
    adapter_rank = cotangent.shape[1]
    languages = lang_embed.shape[0]
    pair_count = src_lang.shape[0]
    lang_ids = jnp.arange(languages, dtype=jnp.int32)
    hot_both = (src_lang[:, None] == lang_ids[None, :]).astype(jnp.float32) + (
        tgt_lang[:, None] == lang_ids[None, :]
    ).astype(jnp.float32)
    pair_embed = jnp.dot(hot_both, lang_embed, precision=lax.Precision.HIGHEST).astype(jnp.bfloat16)
    partial_value = jnp.dot(pair_embed, generator, preferred_element_type=jnp.float32)
    adapter_cols = lax.psum(partial_value, "pair").astype(jnp.bfloat16)
    flat_pairs = block_pair[:, 0]
    row_pairs = lax.dynamic_slice_in_dim(
        flat_pairs, pair_index * (gen_count * blocks_here), gen_count * blocks_here
    )
    send_order = row_pairs.reshape(gen_count, blocks_here).T
    outgoing = jnp.take(adapter_cols, send_order, axis=0).reshape(
        blocks_here, gen_count * adapter_cols.shape[1]
    )
    own_adapters = lax.all_to_all(outgoing, "gen", split_axis=1, concat_axis=1, tiled=True)
    adapters = own_adapters.reshape(blocks_here, model_width, adapter_rank)
    token_blocks = tokens.reshape(blocks_here, BLK, model_width)
    cot_blocks = cotangent.reshape(blocks_here, BLK, adapter_rank)
    hidden = jnp.einsum("btd,bdr->btr", token_blocks, adapters, preferred_element_type=jnp.float32)
    logistic = jax.nn.sigmoid(hidden)
    grad_hidden = (
        cot_blocks.astype(jnp.float32) * logistic * (1.0 + hidden * (1.0 - logistic))
    ).astype(jnp.bfloat16)
    grad_tokens = (
        jnp.einsum("btr,bdr->btd", grad_hidden, adapters, preferred_element_type=jnp.float32)
        .astype(jnp.bfloat16)
        .reshape(tokens.shape)
    )
    outer_grads = jnp.einsum(
        "btd,btr->bdr", token_blocks, grad_hidden, preferred_element_type=jnp.float32
    ).reshape(blocks_here, model_width * adapter_rank)
    returned = lax.all_to_all(outer_grads, "gen", split_axis=1, concat_axis=0, tiled=True)
    pair_ids = jnp.arange(pair_count, dtype=jnp.int32)
    segment_hot = (pair_ids[:, None] == row_pairs[None, :]).astype(jnp.float32)
    row_grad = jnp.dot(segment_hot, returned, precision=lax.Precision.HIGHEST)
    grad_rounded = lax.psum(row_grad, "pair").astype(jnp.bfloat16)
    grad_generator = jnp.einsum(
        "pe,pc->ec", pair_embed, grad_rounded, preferred_element_type=jnp.float32
    ).astype(jnp.bfloat16)
    partial_pair = jnp.einsum(
        "pc,ec->pe", grad_rounded, generator, preferred_element_type=jnp.float32
    )
    grad_pair = lax.psum(partial_pair, "gen")
    grad_embed = jnp.dot(hot_both.T, grad_pair, precision=lax.Precision.HIGHEST)
    return (grad_tokens, grad_generator, grad_embed)


def solution(mesh):
    placed = (
        P(("pair", "gen"), None),
        P(("pair", "gen"), None),
        P(),
        P(),
        P(),
        P(None, "pair"),
        P("pair", "gen"),
    )
    return jax.shard_map(
        shards,
        mesh=mesh,
        in_specs=placed,
        out_specs=(P(("pair", "gen"), None), P("pair", "gen"), P(None, "pair")),
        check_vma=False,
    )
```

profile of v0, /device:TPU:0, one launch (start us, length us, event | category | flops | bytes accessed | tf_op | source)
XLA Modules:
  0.0 421.6 jit_solution(15591775119214140472)
XLA Ops:
  0.6 0.0 copy-start
  0.7 0.7 fusion.16
  1.4 0.7 compare_and_fusion
  2.1 0.0 copy-done
  2.1 0.9 convolution_convert_fusion.2
  3.0 10.1 %fusion.21 = f32[16,65536]{1,0:T(8,128)} fusion(bf16[16,128]{1,0:T(8,128)(2,1)S(1)} %convolution_convert_fusion.2, bf16[128,65536]{1,0:T(8,128)(2,1)} %param.13), kind=kOutput, calls=%fused_computation.39 | convolution fusion | flops 268435456 | bytes 20975616 | tf_op jit(solution)/shard_map/dot_general | solution.py:22
  13.1 149.0 %all-reduce.2 = bf16[16,65536]{1,0:T(8,128)(2,1)S(1)} all-reduce(f32[16,65536]{1,0:T(8,128)} %fusion.21), channel_id=1, replica_groups=mesh['pair'=4,'gen'=8] {'pair'}, use_global_device_ids=true, to_apply=%region_0.0 | all-reduce | flops 1048576 | bytes 6291456 | tf_op jit(solution)/shard_map/psum | solution.py:23
  162.1 1.2 gather_fusion
  163.4 0.2 bitcast_select_fusion
  163.5 1.6 copy.27
  165.2 0.5 broadcast.100
  165.7 7.0 %reduce.2 = bf16[8,65536]{1,0:T(8,128)(2,1)S(1)} reduce(bf16[8,1,65536]{2,1,0:T(2,128)(2,1)S(1)} %bitcast.33, bf16[]{:T(256)} %broadcast.100), dimensions={1}, to_apply=%bitcast.32.reduce_sub_computation | reduce | bytes 2097154
  172.7 0.0 copy-start.4
  172.7 1.9 reshape.166
  174.6 3.8 all-to-all-start
  178.4 0.0 copy-done.4
  178.4 1.0 copy.17
  179.4 14.3 %all-to-all-done = bf16[8,2,32768]{2,1,0:T(2,128)(2,1)S(1)} async-done(((bf16[8,2,32768]{2,1,0:T(2,128)(2,1)}), bf16[8,2,32768]{2,1,0:T(2,128)(2,1)S(1)}, u32[]{:S(2)}, u32[]{:S(2)}) %all-to-all-start) | async-done | bytes 1048608 | tf_op jit(solution)/shard_map/all_to_all | solution.py:32
  193.7 1.0 reshape.167
  194.8 6.0 %bitcast_reduce_fusion = bf16[8,65536]{1,0:T(8,128)(2,1)S(1)} fusion(bf16[8,1,65536]{2,1,0:T(2,128)(2,1)S(1)} %reshape.167), kind=kLoop, calls=%fused_computation.37 | loop fusion | bytes 2097152 | tf_op jit(solution)/shard_map/all_to_all | solution.py:32
  200.8 0.5 reshape.156
  201.3 0.0 copy-start.2
  201.3 0.0 copy-start.5
  201.3 0.0 copy-start.6
  201.3 3.9 convolution_bitcast_fusion.1
  205.2 0.0 copy-done.2
  205.2 0.0 copy-start.9
  205.2 1.0 copy-done.9
  206.2 0.0 copy-done.5
  206.2 0.0 copy-done.6
  206.2 2.9 convolution_bitcast_fusion
  209.1 1.9 copy.19
  211.0 0.0 copy-start.3
  211.0 4.2 all_to_all.20
  215.2 3.9 all-to-all-start.1
  219.0 0.0 copy-done.3
  219.0 5.0 %convolution_convert_fusion.1 = bf16[1024,2048]{1,0:T(8,128)(2,1)} fusion(bf16[2048,256]{1,0:T(8,128)(2,1)S(1)} %copy-done.3, f32[1024,256]{0,1:T(8,128)} %copy-done.9, bf16[1024,256]{0,1:T(8,128)(2,1)} %copy.17), kind=kOutput, calls=%fused_computation.2 | convolution fusion | flops 1078460416 | bytes 6815744 | tf_op jit(solution)/shard_map/btr,bdr->btd/dot_general | solution.py:42
  224.0 21.3 %all-to-all-done.1 = f32[1,8,65536]{2,0,1:T(1,128)S(1)} async-done(((f32[1,8,65536]{2,0,1:T(1,128)}), f32[1,8,65536]{2,0,1:T(1,128)S(1)}, u32[]{:S(2)}, u32[]{:S(2)}) %all-to-all-start.1) | async-done | bytes 2097184 | tf_op jit(solution)/shard_map/all_to_all | solution.py:49
  245.3 4.8 %fusion = f32[16,65536]{1,0:T(8,128)} fusion(f32[1,8,65536]{2,0,1:T(1,128)S(1)} %all-to-all-done.1, s32[8]{0:T(128)S(1)} %get-tuple-element.4), kind=kOutput, calls=%fused_computation.4 | convolution fusion | flops 100663424 | bytes 6291488 | tf_op jit(solution)/shard_map/dot_general | solution.py:52
  250.1 141.2 %all-reduce.3 = bf16[16,65536]{1,0:T(8,128)(2,1)S(1)} all-reduce(f32[16,65536]{1,0:T(8,128)} %fusion), channel_id=1, replica_groups=mesh['pair'=4,'gen'=8] {'pair'}, use_global_device_ids=true, to_apply=%region_1.2 | all-reduce | flops 1048576 | bytes 6291456 | tf_op jit(solution)/shard_map/psum | solution.py:53
  391.4 8.5 %convolution_convert_fusion = bf16[128,65536]{1,0:T(8,128)(2,1)} fusion(bf16[16,128]{1,0:T(8,128)(2,1)S(1)} %convolution_convert_fusion.2, bf16[16,65536]{1,0:T(8,128)(2,1)S(1)} %all-reduce.3), kind=kOutput, calls=%fused_computation.1 | convolution fusion | flops 276824064 | bytes 18878464 | tf_op jit(solution)/shard_map/pe,pc->ec/dot_general | solution.py:54
  399.9 0.0 copy-start.7
  399.9 0.0 copy-start.8
  399.9 0.0 copy-start.1
  399.9 8.1 %fusion.22 = f32[16,128]{1,0:T(8,128)S(1)} fusion(bf16[16,65536]{1,0:T(8,128)(2,1)S(1)} %all-reduce.3, bf16[128,65536]{1,0:T(8,128)(2,1)} %param.13), kind=kOutput, calls=%fused_computation.40 | convolution fusion | flops 268435456 | bytes 18882560 | tf_op jit(solution)/shard_map/pc,ec->pe/dot_general | solution.py:57
  408.0 12.6 %psum.23 = f32[16,128]{1,0:T(8,128)S(1)} all-reduce(f32[16,128]{1,0:T(8,128)S(1)} %fusion.22), channel_id=1, replica_groups=mesh['pair'=4,'gen'=8] {'gen'}, use_global_device_ids=true, to_apply=%region_2.3 | all-reduce | flops 2048 | bytes 16384 | tf_op jit(solution)/shard_map/psum | solution.py:60
  420.6 0.0 copy-done.7
  420.6 0.0 copy-done.8
  420.6 1.0 fusion.10
  421.6 0.0 copy-done.1
  (1 shorter events, 0.0 us)
Async XLA Ops:
  0.6 1.5 copy-start
  172.7 5.7 %copy-start.4 = (bf16[1024,256]{1,0:T(8,128)(2,1)S(1)}, bf16[1024,256]{1,0:T(8,128)(2,1)}, u32[]{:S(2)}) copy-start(bf16[1024,256]{1,0:T(8,128)(2,1)} %param.8) | copy-start | bytes 1572868
  174.6 19.1 %all-to-all-start = ((bf16[8,2,32768]{2,1,0:T(2,128)(2,1)}), bf16[8,2,32768]{2,1,0:T(2,128)(2,1)S(1)}, u32[]{:S(2)}, u32[]{:S(2)}) async-start(bf16[8,2,32768]{2,1,0:T(2,128)(2,1)} %reshape.166), calls=%async_computation | async-start | bytes 2097152 | tf_op jit(solution)/shard_map/all_to_all | solution.py:32
  201.3 3.9 copy-start.2
  201.3 4.9 %copy-start.5 = (bf16[1024,256]{0,1:T(8,128)(2,1)S(1)}, bf16[1024,256]{0,1:T(8,128)(2,1)}, u32[]{:S(2)}) copy-start(bf16[1024,256]{0,1:T(8,128)(2,1)} %copy.17) | copy-start | bytes 1572868
  201.3 4.9 %copy-start.6 = (bf16[1024,2048]{1,0:T(8,128)(2,1)S(1)}, bf16[1024,2048]{1,0:T(8,128)(2,1)}, u32[]{:S(2)}) copy-start(bf16[1024,2048]{1,0:T(8,128)(2,1)} %param.7) | copy-start | bytes 12582916
  205.2 1.0 copy-start.9
  211.0 8.0 %copy-start.3 = (bf16[2048,256]{1,0:T(8,128)(2,1)S(1)}, bf16[2048,256]{1,0:T(8,128)(2,1)}, u32[]{:S(2)}) copy-start(bf16[2048,256]{1,0:T(8,128)(2,1)} %copy-done.2) | copy-start | bytes 3145732
  215.2 30.2 %all-to-all-start.1 = ((f32[1,8,65536]{2,0,1:T(1,128)}), f32[1,8,65536]{2,0,1:T(1,128)S(1)}, u32[]{:S(2)}, u32[]{:S(2)}) async-start(f32[1,8,65536]{2,0,1:T(1,128)} %all_to_all.20), calls=%async_computation.1 | async-start | bytes 4194304 | tf_op jit(solution)/shard_map/all_to_all | solution.py:49
  399.9 20.7 %copy-start.7 = (s32[16]{0:T(128)S(1)}, s32[16]{0:T(128)}, u32[]{:S(2)}) copy-start(s32[16]{0:T(128)} %param.11) | copy-start | bytes 196
  399.9 20.7 %copy-start.8 = (s32[16]{0:T(128)S(1)}, s32[16]{0:T(128)}, u32[]{:S(2)}) copy-start(s32[16]{0:T(128)} %param.10) | copy-start | bytes 196
  399.9 21.7 %copy-start.1 = (f32[96,128]{1,0:T(8,128)S(1)}, f32[96,128]{1,0:T(8,128)}, u32[]{:S(2)}) copy-start(f32[96,128]{1,0:T(8,128)} %param.12) | copy-start | bytes 147460
where the time goes:
time: 422 us
  blocking collectives  303 us (72%)
  matrix products  45.1 us (11%)
  waiting for transfers between devices  35.7 us (8%)
  local copies, waits for them, and re-layouts  20.8 us (5%)
  other arithmetic  8.67 us (2%)
  starting transfers between devices  7.64 us (2%)
    psum x1, blocking collectives, shards(): adapter_cols = lax.psum(partial_value, 'pair').astype(jnp.bfloat16)  149 us
    psum x1, blocking collectives, shards(): grad_rounded = lax.psum(row_grad, 'pair').astype(jnp.bfloat16)  141 us
    all_to_all x1, waiting for transfers between devices, shards(): lax.all_to_all(outer_grads, 'gen', split_axis=1, concat_axis=0, tiled=True)  21.3 us
    all_to_all x1, waiting for transfers between devices, shards(): lax.all_to_all(outgoing, 'gen', split_axis=1, concat_axis=1, tiled=True)  14.3 us
    psum x1, blocking collectives, shards(): grad_pair = lax.psum(partial_pair, 'gen')  12.6 us
    dot_general x1, matrix products, shards(): jnp.dot(pair_embed, generator, preferred_element_type=jnp.float32)  10.1 us
    dot_general x1, matrix products, shards(): jnp.einsum('pe,pc->ec', pair_embed, grad_rounded, preferred_element_type=...  8.55 us
  transfers between devices with their start and end apart: 2, of which 2 were waited for; matrix products, arithmetic and copies ran while one was open for 1% of the time, Pallas kernels for 0%

commit v1 on v0

--- a/solution.py
+++ b/solution.py
@@ -46,7 +46,12 @@
     outer_grads = jnp.einsum(
         "btd,btr->bdr", token_blocks, grad_hidden, preferred_element_type=jnp.float32
     ).reshape(blocks_here, model_width * adapter_rank)
-    returned = lax.all_to_all(outer_grads, "gen", split_axis=1, concat_axis=0, tiled=True)
+    returned = jnp.concatenate(
+        lax.all_to_all(
+            jnp.stack(jnp.split(outer_grads, lax.axis_size("gen"), axis=1)), "gen", 0, 0
+        ),
+        axis=0,
+    )
     pair_ids = jnp.arange(pair_count, dtype=jnp.int32)
     segment_hot = (pair_ids[:, None] == row_pairs[None, :]).astype(jnp.float32)
     row_grad = jnp.dot(segment_hot, returned, precision=lax.Precision.HIGHEST)

time: 422 us -> 432 us (1.024)
  local copies, waits for them, and re-layouts: 20.8 us -> 31 us
    unnamed x24 -> x28, local copies, waits for them, and re-layouts: 5.44 us -> 19.1 us
where the time goes in v1:
time: 432 us
  blocking collectives  303 us (70%)
  matrix products  44.8 us (10%)
  waiting for transfers between devices  35.6 us (8%)
  local copies, waits for them, and re-layouts  31 us (7%)
  other arithmetic  8.67 us (2%)
  starting transfers between devices  7.64 us (2%)
    psum x1, blocking collectives, shards(): adapter_cols = lax.psum(partial_value, 'pair').astype(jnp.bfloat16)  149 us
    psum x1, blocking collectives, shards(): grad_rounded = lax.psum(row_grad, 'pair').astype(jnp.bfloat16)  142 us
    all_to_all x1, waiting for transfers between devices, shards(): lax.all_to_all(jnp.stack(jnp.split(outer_grads, lax.axis_size('gen'), axi...  21.3 us
    unnamed x28, local copies, waits for them, and re-layouts  19.1 us
    all_to_all x1, waiting for transfers between devices, shards(): lax.all_to_all(outgoing, 'gen', split_axis=1, concat_axis=1, tiled=True)  14.3 us
    psum x1, blocking collectives, shards(): grad_pair = lax.psum(partial_pair, 'gen')  12 us
    dot_general x1, matrix products, shards(): jnp.dot(pair_embed, generator, preferred_element_type=jnp.float32)  10.1 us
  transfers between devices with their start and end apart: 2, of which 2 were waited for; matrix products, arithmetic and copies ran while one was open for 1% of the time, Pallas kernels for 0%

profile of v1, /device:TPU:0, one launch (start us, length us, event | category | flops | bytes accessed | tf_op | source)
XLA Modules:
  0.0 431.7 jit_solution(16448050527717580973)
XLA Ops:
  0.6 0.0 copy-start
  0.7 0.7 fusion.24
  1.4 0.7 compare_and_fusion
  2.1 0.0 copy-done
  2.1 0.9 convolution_convert_fusion.2
  3.0 10.1 %fusion.29 = f32[16,65536]{1,0:T(8,128)} fusion(bf16[16,128]{1,0:T(8,128)(2,1)S(1)} %convolution_convert_fusion.2, bf16[128,65536]{1,0:T(8,128)(2,1)} %param.13), kind=kOutput, calls=%fused_computation.55 | convolution fusion | flops 268435456 | bytes 20975616 | tf_op jit(solution)/shard_map/dot_general | solution.py:22
  13.1 149.0 %all-reduce.2 = bf16[16,65536]{1,0:T(8,128)(2,1)S(1)} all-reduce(f32[16,65536]{1,0:T(8,128)} %fusion.29), channel_id=1, replica_groups=mesh['pair'=4,'gen'=8] {'pair'}, use_global_device_ids=true, to_apply=%region_0.0 | all-reduce | flops 1048576 | bytes 6291456 | tf_op jit(solution)/shard_map/psum | solution.py:23
  162.1 1.2 gather_fusion
  163.4 0.2 bitcast_select_fusion
  163.5 1.6 copy.26
  165.2 0.5 broadcast.100
  165.7 7.0 %reduce.2 = bf16[8,65536]{1,0:T(8,128)(2,1)S(1)} reduce(bf16[8,1,65536]{2,1,0:T(2,128)(2,1)S(1)} %bitcast.76, bf16[]{:T(256)} %broadcast.100), dimensions={1}, to_apply=%bitcast.67.reduce_sub_computation | reduce | bytes 2097154
  172.7 0.0 copy-start.2
  172.7 1.9 reshape.166
  174.6 3.8 all-to-all-start
  178.4 0.0 copy-done.2
  178.4 1.0 copy.16
  179.4 14.3 %all-to-all-done = bf16[8,2,32768]{2,1,0:T(2,128)(2,1)S(1)} async-done(((bf16[8,2,32768]{2,1,0:T(2,128)(2,1)}), bf16[8,2,32768]{2,1,0:T(2,128)(2,1)S(1)}, u32[]{:S(2)}, u32[]{:S(2)}) %all-to-all-start) | async-done | bytes 1048608 | tf_op jit(solution)/shard_map/all_to_all | solution.py:32
  193.7 1.0 reshape.167
  194.8 6.0 %bitcast_reduce_fusion = bf16[8,65536]{1,0:T(8,128)(2,1)S(1)} fusion(bf16[8,1,65536]{2,1,0:T(2,128)(2,1)S(1)} %reshape.167), kind=kLoop, calls=%fused_computation.53 | loop fusion | bytes 2097152 | tf_op jit(solution)/shard_map/all_to_all | solution.py:32
  200.8 0.5 reshape.154
  201.3 0.0 copy-start.3
  201.3 0.0 copy-start.4
  201.3 3.6 convolution_bitcast_fusion.1
  204.9 0.0 copy-start.7
  204.9 1.0 copy-done.7
  205.9 0.0 copy-done.3
  205.9 0.0 copy-done.4
  205.9 2.8 convolution_bitcast_fusion
  208.7 1.9 copy.18
  210.7 8.6 %copy.20 = f32[1,1,2048,256]{3,1,2,0:T(1,128)S(1)} copy(f32[1,1,2048,256]{3,2,1,0:T(8,128)S(1)} %bitcast.77) | data formatting | bytes 4194304
  219.2 0.7 fusion.17
  220.0 0.7 fusion.16
  220.7 0.7 fusion.15
  221.4 0.7 fusion.14
  222.1 0.7 fusion.13
  222.8 0.7 fusion.12
  223.6 0.7 fusion.11
  224.3 0.7 fusion.10
  225.0 3.9 all-to-all-start.1
  228.9 5.0 %convolution_convert_fusion.1 = bf16[1024,2048]{1,0:T(8,128)(2,1)} fusion(bf16[2048,256]{1,0:T(8,128)(2,1)S(1)} %reshape.154, f32[1024,256]{0,1:T(8,128)} %copy-done.7, bf16[1024,256]{0,1:T(8,128)(2,1)} %copy.16), kind=kOutput, calls=%fused_computation.2 | convolution fusion | flops 1078460416 | bytes 6815744 | tf_op jit(solution)/shard_map/btr,bdr->btd/dot_general | solution.py:42
  233.9 21.3 %all-to-all-done.1 = f32[8,1,65536]{2,1,0:T(1,128)S(1)} async-done(((f32[8,1,65536]{2,1,0:T(1,128)}), f32[8,1,65536]{2,1,0:T(1,128)S(1)}, u32[]{:S(2)}, u32[]{:S(2)}) %all-to-all-start.1) | async-done | bytes 2097184 | tf_op jit(solution)/shard_map/all_to_all | solution.py:50
  255.2 4.8 %fusion = f32[16,65536]{1,0:T(8,128)} fusion(f32[8,1,65536]{2,1,0:T(1,128)S(1)} %all-to-all-done.1, s32[8]{0:T(128)S(1)} %get-tuple-element.4), kind=kOutput, calls=%fused_computation.4 | convolution fusion | flops 100663424 | bytes 6291488 | tf_op jit(solution)/shard_map/dot_general | solution.py:57
  260.0 142.1 %all-reduce.3 = bf16[16,65536]{1,0:T(8,128)(2,1)S(1)} all-reduce(f32[16,65536]{1,0:T(8,128)} %fusion), channel_id=1, replica_groups=mesh['pair'=4,'gen'=8] {'pair'}, use_global_device_ids=true, to_apply=%region_1.2 | all-reduce | flops 1048576 | bytes 6291456 | tf_op jit(solution)/shard_map/psum | solution.py:58
  402.1 8.5 %convolution_convert_fusion = bf16[128,65536]{1,0:T(8,128)(2,1)} fusion(bf16[16,128]{1,0:T(8,128)(2,1)S(1)} %convolution_convert_fusion.2, bf16[16,65536]{1,0:T(8,128)(2,1)S(1)} %all-reduce.3), kind=kOutput, calls=%fused_computation.1 | convolution fusion | flops 276824064 | bytes 18878464 | tf_op jit(solution)/shard_map/pe,pc->ec/dot_general | solution.py:59
  410.6 0.0 copy-start.5
  410.6 0.0 copy-start.6
  410.6 0.0 copy-start.1
  410.6 8.1 %fusion.30 = f32[16,128]{1,0:T(8,128)S(1)} fusion(bf16[16,65536]{1,0:T(8,128)(2,1)S(1)} %all-reduce.3, bf16[128,65536]{1,0:T(8,128)(2,1)} %param.13), kind=kOutput, calls=%fused_computation.56 | convolution fusion | flops 268435456 | bytes 18882560 | tf_op jit(solution)/shard_map/pc,ec->pe/dot_general | solution.py:62
  418.7 12.0 %psum.23 = f32[16,128]{1,0:T(8,128)S(1)} all-reduce(f32[16,128]{1,0:T(8,128)S(1)} %fusion.30), channel_id=1, replica_groups=mesh['pair'=4,'gen'=8] {'gen'}, use_global_device_ids=true, to_apply=%region_2.3 | all-reduce | flops 2048 | bytes 16384 | tf_op jit(solution)/shard_map/psum | solution.py:65
  430.8 0.0 copy-done.5
  430.8 0.0 copy-done.6
  430.8 1.0 fusion.18
  431.7 0.0 copy-done.1
  (1 shorter events, 0.0 us)
Async XLA Ops:
  0.6 1.5 copy-start
  172.7 5.7 %copy-start.2 = (bf16[1024,256]{1,0:T(8,128)(2,1)S(1)}, bf16[1024,256]{1,0:T(8,128)(2,1)}, u32[]{:S(2)}) copy-start(bf16[1024,256]{1,0:T(8,128)(2,1)} %param.8) | copy-start | bytes 1572868
  174.6 19.1 %all-to-all-start = ((bf16[8,2,32768]{2,1,0:T(2,128)(2,1)}), bf16[8,2,32768]{2,1,0:T(2,128)(2,1)S(1)}, u32[]{:S(2)}, u32[]{:S(2)}) async-start(bf16[8,2,32768]{2,1,0:T(2,128)(2,1)} %reshape.166), calls=%async_computation | async-start | bytes 2097152 | tf_op jit(solution)/shard_map/all_to_all | solution.py:32
  201.3 4.7 %copy-start.3 = (bf16[1024,256]{0,1:T(8,128)(2,1)S(1)}, bf16[1024,256]{0,1:T(8,128)(2,1)}, u32[]{:S(2)}) copy-start(bf16[1024,256]{0,1:T(8,128)(2,1)} %copy.16) | copy-start | bytes 1572868
  201.3 4.6 %copy-start.4 = (bf16[1024,2048]{1,0:T(8,128)(2,1)S(1)}, bf16[1024,2048]{1,0:T(8,128)(2,1)}, u32[]{:S(2)}) copy-start(bf16[1024,2048]{1,0:T(8,128)(2,1)} %param.7) | copy-start | bytes 12582916
  204.9 1.0 copy-start.7
  225.0 30.2 %all-to-all-start.1 = ((f32[8,1,65536]{2,1,0:T(1,128)}), f32[8,1,65536]{2,1,0:T(1,128)S(1)}, u32[]{:S(2)}, u32[]{:S(2)}) async-start(f32[8,1,65536]{2,1,0:T(1,128)} %fusion.10), calls=%async_computation.1 | async-start | bytes 4194304 | tf_op jit(solution)/shard_map/all_to_all | solution.py:50
  410.6 20.1 %copy-start.5 = (s32[16]{0:T(128)S(1)}, s32[16]{0:T(128)}, u32[]{:S(2)}) copy-start(s32[16]{0:T(128)} %param.11) | copy-start | bytes 196
  410.6 20.1 %copy-start.6 = (s32[16]{0:T(128)S(1)}, s32[16]{0:T(128)}, u32[]{:S(2)}) copy-start(s32[16]{0:T(128)} %param.10) | copy-start | bytes 196
  410.6 21.1 %copy-start.1 = (f32[96,128]{1,0:T(8,128)S(1)}, f32[96,128]{1,0:T(8,128)}, u32[]{:S(2)}) copy-start(f32[96,128]{1,0:T(8,128)} %param.12) | copy-start | bytes 147460
